TPU v7x, 512 devices: a whole 4x4x16 slice. The times are simulated.
512 devices in a mesh: dp: 32 (over z, core), cent: 16 (over y, x).
Axes of the slice: x: 4, y: 4, z: 16, core: 2. Of those that a mesh axis runs over, the one named last changes fastest.
Arguments:
- points: bfloat16 [131072, 1024], P(('dp', 'cent')), may hold values from -22 to 22, as said below
- block_list: int32 [4096, 3], P(('dp', 'cent')), may hold values from 0 to 15, all different within a row; in each aligned block of 8 rows (0 to 7, 8 to 15, ...) at most 2 rows name the same one
- list_count: int32 [4096], P(('dp', 'cent')), may hold values from 1 to 3
- centroids: bfloat16 [16, 1024, 1024], P('cent', 'dp'), may hold values from -14 to 14, as said below
Outputs:
- new_centroids: float32 [16, 1024, 1024], P('cent', 'dp')
Inputs may be any that keep to these rules, and one draw needn't show every extreme that they name: `block_list`: within the rows of one device (aligned blocks of 8 rows) no block id appears more than 2 times, and the ids of one row differ. Only the first list_count[t] entries of row t of block_list are valid. `points`: Real-valued embeddings. Real-valued centroids.
All inputs are finite; a program needn't handle non-finite values.
Results may differ from a plain program's by a relative error of at most 0.0019.
Values may be sent and summed in bfloat16 or wider, within the bound.
No kernel may reach another device: no remote copies, remote signals or barrier semaphores. Data moves between devices by JAX's collectives and lax.ppermute only.
A program may use at most 64 MiB of HBM per device.

v0:
```python
import math
import jax
import jax.numpy as jnp
from jax import lax
from jax.sharding import PartitionSpec as P

score_scale = 2.0
prior_weight = 1.0
empty_norm = 1e30


def combine_norms(peaks, totals, usable):
    keep = usable[..., None]
    highest = jnp.max(jnp.where(keep, peaks, -1e30), axis=-2)
    summed = jnp.sum(jnp.where(keep, totals * jnp.exp(peaks - highest[..., None, :]), 0.0), axis=-2)
    return highest + jnp.log(summed)


def per_device(points, block_list, list_count, centroids):
    owners = lax.axis_size("cent")
    tiles_here, listed = block_list.shape
    width = points.shape[1]
    tile_rows = points.shape[0] // tiles_here
    capacity = (tiles_here * listed + owners - 1) // owners
    slot_rows = capacity * tile_rows
    scale = score_scale / math.sqrt(width)
    usable = jnp.arange(listed, dtype=jnp.int32)[None, :] < list_count[:, None]
    naming = jnp.logical_and(
        block_list[:, :, None] == jnp.arange(owners, dtype=jnp.int32)[None, None, :],
        usable[:, :, None],
    )
    listing = jnp.any(naming, axis=1).astype(jnp.int32)
    earlier = jnp.cumsum(listing, axis=0) - listing
    placing = jnp.logical_and(
        listing.T[:, None, :] == 1,
        earlier.T[:, None, :] == jnp.arange(capacity, dtype=jnp.int32)[None, :, None],
    )
    placing = placing.astype(jnp.float32).reshape(owners * capacity, tiles_here)
    slot_rank = jnp.take_along_axis(earlier, block_list, axis=1)
    route_code = jnp.where(usable, block_list * capacity + slot_rank, -1)
    outgoing = jnp.dot(
        placing.astype(jnp.bfloat16),
        points.reshape(tiles_here, tile_rows * width),
        preferred_element_type=jnp.float32,
    )
    outgoing = outgoing.astype(jnp.bfloat16).reshape(owners, slot_rows, width)
    arrived = lax.all_to_all(outgoing, "cent", split_axis=0, concat_axis=0, tiled=True)
    incoming = arrived.reshape(owners * slot_rows, width)
    logits = (
        lax.dot_general(
            incoming,
            lax.all_gather(centroids, "dp", axis=1, tiled=True)[0],
            (((1,), (1,)), ((), ())),
            preferred_element_type=jnp.float32,
        )
        * scale
    )
    peaks = jnp.max(logits, axis=1)
    totals = jnp.sum(jnp.exp(logits - peaks[:, None]), axis=1)
    stats = jnp.stack([peaks.reshape(owners, slot_rows), totals.reshape(owners, slot_rows)], axis=1)
    back = lax.all_to_all(stats, "cent", split_axis=0, concat_axis=0, tiled=True)
    back_peaks = back[:, 0].reshape(owners * capacity, tile_rows)
    back_totals = back[:, 1].reshape(owners * capacity, tile_rows)
    lookup = jnp.where(usable, route_code, 0)
    tile_norms = combine_norms(back_peaks[lookup], back_totals[lookup], usable)
    empty = 1.0 - jnp.sum(placing, axis=1)
    slot_norms = (
        jnp.dot(placing, tile_norms, precision=lax.Precision.HIGHEST) + empty[:, None] * empty_norm
    )
    row_norms = lax.all_to_all(
        slot_norms.reshape(owners, slot_rows), "cent", split_axis=0, concat_axis=0, tiled=True
    ).reshape(-1)
    shares = jnp.exp(logits - row_norms[:, None]).astype(jnp.bfloat16)
    own_rows = centroids[0].astype(jnp.float32)
    marker = (jnp.arange(128, dtype=jnp.int32) == 0).astype(jnp.bfloat16)
    widened = jnp.concatenate(
        [incoming, jnp.broadcast_to(marker[None, :], (incoming.shape[0], 128))], axis=1
    )
    block_sums = lax.dot_general(
        shares, widened, (((0,), (0,)), ((), ())), preferred_element_type=jnp.float32
    )
    reduced = lax.psum_scatter(block_sums, "dp", scatter_dimension=0, tiled=True)
    new_sums = reduced[:, :width]
    new_mass = reduced[:, width]
    fresh = (new_sums + prior_weight * own_rows) / (new_mass[:, None] + prior_weight)
    return fresh[None]


def solution(mesh):
    in_specs = (
        P(("dp", "cent"), None),
        P(("dp", "cent"), None),
        P(("dp", "cent")),
        P("cent", "dp", None),
    )
    out_specs = P("cent", "dp", None)
    return jax.shard_map(
        per_device, mesh=mesh, in_specs=in_specs, out_specs=out_specs, check_vma=False
    )
```

profile of v0, /device:TPU:4, one launch (start us, length us, event | category | flops | bytes accessed | tf_op | source)
XLA Modules:
  0.0 250.5 jit_solution(18403319197507277494)
XLA Ops:
  6.5 0.7 all-gather.2.cloned.1.call-update
  7.3 0.7 iota_compare_fusion.1
  8.1 0.8 fusion.16
  9.1 1.3 reshape.116
  10.4 0.7 convolution_convert_fusion
  11.1 2.4 reshape.117
  13.4 9.5 %all-to-all-start = ((bf16[16,64,1024]{2,1,0:T(8,128)(2,1)}), bf16[16,64,1024]{2,1,0:T(8,128)(2,1)S(1)}, u32[]{:S(2)}, u32[]{:S(2)}) async-start(bf16[16,64,1024]{2,1,0:T(8,128)(2,1)} %reshape.117), calls=%async_computation | async-start | bytes 4194304 | tf_op jit(solution)/shard_map/all_to_all | solution.py:47
  23.3 0.7 gather_fusion.2
  24.4 22.4 %all-to-all-done = bf16[16,64,1024]{2,1,0:T(8,128)(2,1)S(1)} async-done(((bf16[16,64,1024]{2,1,0:T(8,128)(2,1)}), bf16[16,64,1024]{2,1,0:T(8,128)(2,1)S(1)}, u32[]{:S(2)}, u32[]{:S(2)}) %all-to-all-start) | async-done | bytes 2097184 | tf_op jit(solution)/shard_map/all_to_all | solution.py:47
  46.8 39.0 %all-gather.2.cloned.1.call-done = bf16[1,1024,1024]{2,1,0:T(8,128)(2,1)} async-done(((bf16[1,32,1024]{2,1,0:T(8,128)(2,1)}), bf16[1,1024,1024]{2,1,0:T(8,128)(2,1)}) %all-gather.2.cloned.1.call-update) | async-done | bytes 2097168 | tf_op jit(solution)/shard_map/all_gather | solution.py:52
  85.8 6.0 %multiply_reduce_fusion = (f32[1024]{0:T(1024)S(1)}, f32[1024,1024]{0,1:T(8,128)}) fusion(bf16[1024,1024]{1,0:T(8,128)(2,1)S(1)} %bitcast.25, bf16[1,1024,1024]{2,1,0:T(8,128)(2,1)} %all-gather.2.cloned.1.call-done), kind=kOutput, calls=%fused_computation.6 | convolution fusion | flops 2149579776 | bytes 8392704 | tf_op jit(solution)/shard_map/dot_general | solution.py:50
  91.8 2.9 %exponential_reduce_fusion = f32[1024]{0:T(1024)S(1)} fusion(f32[1024,1024]{0,1:T(8,128)} %get-tuple-element.10, f32[1024]{0:T(1024)S(1)} %get-tuple-element.9), kind=kLoop, calls=%fused_computation.5 | loop fusion | flops 3144704 | bytes 4202496 | tf_op jit(solution)/shard_map/reduce_sum | solution.py:59
  94.8 0.7 reshape.173
  95.5 7.2 %all-to-all-start.1 = ((f32[16,1,128]{2,1,0:T(1,128)}), f32[16,1,128]{2,1,0:T(1,128)S(1)}, u32[]{:S(2)}, u32[]{:S(2)}) async-start(f32[16,1,128]{2,1,0:T(1,128)} %reshape.173), calls=%async_computation.1 | async-start | bytes 16384 | tf_op jit(solution)/shard_map/all_to_all | solution.py:61
  103.0 5.0 %all-to-all-done.1 = f32[16,1,128]{2,1,0:T(1,128)S(1)} async-done(((f32[16,1,128]{2,1,0:T(1,128)}), f32[16,1,128]{2,1,0:T(1,128)S(1)}, u32[]{:S(2)}, u32[]{:S(2)}) %all-to-all-start.1) | async-done | bytes 8224 | tf_op jit(solution)/shard_map/all_to_all | solution.py:61
  108.5 0.7 reduce.15
  111.0 0.7 all_to_all.14
  111.7 5.6 %all-to-all-start.2 = ((f32[16,1,64]{2,1,0:T(1,128)}), f32[16,1,64]{2,1,0:T(1,128)S(1)}, u32[]{:S(2)}, u32[]{:S(2)}) async-start(f32[16,1,64]{2,1,0:T(1,128)} %bitcast.7), calls=%async_computation.2 | async-start | bytes 16384 | tf_op jit(solution)/shard_map/all_to_all | solution.py:70
  117.4 5.2 %all-to-all-done.2 = f32[16,1,64]{2,1,0:T(1,128)S(1)} async-done(((f32[16,1,64]{2,1,0:T(1,128)}), f32[16,1,64]{2,1,0:T(1,128)S(1)}, u32[]{:S(2)}, u32[]{:S(2)}) %all-to-all-start.2) | async-done | bytes 4128 | tf_op jit(solution)/shard_map/all_to_all | solution.py:70
  123.1 0.7 reduce.14
  123.9 7.4 %fusion = f32[1024,1152]{1,0:T(8,128)} fusion(bf16[1024,1024]{1,0:T(8,128)(2,1)S(1)} %bitcast.26, f32[1024,1024]{0,1:T(8,128)} %get-tuple-element.10, f32[1024]{0:T(1024)S(1)} %sub.54, bf16[1152]{0:T(1024)(128)(2,1)S(1)} %pad.1.clone), kind=kOutput, calls=%fused_computation.7 | convolution fusion | flops 2423783424 | bytes 11016448 | tf_op jit(solution)/shard_map/dot_general | solution.py:79
  131.3 109.9 %reduce-scatter.2.cloned.1.call-done = f32[32,1152]{1,0:T(8,128)} async-done(((f32[1024,1152]{1,0:T(8,128)}), f32[32,1152]{1,0:T(8,128)}) %reduce-scatter.2.cloned.1.call-update) | async-done | bytes 147472 | tf_op jit(solution)/shard_map/reduce_scatter | solution.py:82
  241.2 0.8 fusion.10
  242.0 1.6 fusion.9
  (53 shorter events, 4.4 us)
Async XLA Ops:
  6.5 79.2 %all-gather.2.cloned.1.call-start = ((), (), s32[]{:S(2)}) async-start(), calls=%async_computation.4 | async-start | bytes 2162688 | tf_op jit(solution)/shard_map/all_gather | solution.py:52
  11.0 11.9 %copy-start.1 = (s32[8,3]{0,1:T(4,128)S(1)}, s32[8,3]{0,1:T(4,128)}, u32[]{:S(2)}) copy-start(s32[8,3]{0,1:T(4,128)} %param.5) | copy-start | bytes 292
  13.4 10.7 %copy-start.2 = (s32[8]{0:T(128)S(1)}, s32[8]{0:T(128)}, u32[]{:S(2)}) copy-start(s32[8]{0:T(128)} %param.6) | copy-start | bytes 100
  13.4 33.3 %all-to-all-start = ((bf16[16,64,1024]{2,1,0:T(8,128)(2,1)}), bf16[16,64,1024]{2,1,0:T(8,128)(2,1)S(1)}, u32[]{:S(2)}, u32[]{:S(2)}) async-start(bf16[16,64,1024]{2,1,0:T(8,128)(2,1)} %reshape.117), calls=%async_computation | async-start | bytes 4194304 | tf_op jit(solution)/shard_map/all_to_all | solution.py:47
  95.5 12.5 %all-to-all-start.1 = ((f32[16,1,128]{2,1,0:T(1,128)}), f32[16,1,128]{2,1,0:T(1,128)S(1)}, u32[]{:S(2)}, u32[]{:S(2)}) async-start(f32[16,1,128]{2,1,0:T(1,128)} %reshape.173), calls=%async_computation.1 | async-start | bytes 16384 | tf_op jit(solution)/shard_map/all_to_all | solution.py:61
  111.7 10.9 %all-to-all-start.2 = ((f32[16,1,64]{2,1,0:T(1,128)}), f32[16,1,64]{2,1,0:T(1,128)S(1)}, u32[]{:S(2)}, u32[]{:S(2)}) async-start(f32[16,1,64]{2,1,0:T(1,128)} %bitcast.7), calls=%async_computation.2 | async-start | bytes 16384 | tf_op jit(solution)/shard_map/all_to_all | solution.py:70
  117.3 123.8 %reduce-scatter.2.cloned.1.call-start = ((), (), s32[]{:S(2)}) async-start(), calls=%async_computation.5 | async-start | bytes 4866048 | tf_op jit(solution)/shard_map/reduce_scatter | solution.py:82
  131.3 110.7 %copy-start = (bf16[1,32,1024]{2,1,0:T(8,128)(2,1)S(1)}, bf16[1,32,1024]{2,1,0:T(8,128)(2,1)}, u32[]{:S(2)}) copy-start(bf16[1,32,1024]{2,1,0:T(8,128)(2,1)} %param.7) | copy-start | bytes 196612
Sparse Core Ops, SparseCore 0:
  9.5 76.2 all-gather.1
  131.4 109.7 reduce-scatter.1
where the time goes:
time: 251 us; the launch traced here: 250 us
  waiting for transfers between devices  182 us (73%)
  starting transfers between devices  22.4 us (9%)
  matrix products  14.2 us (6%)
  between operations  13.6 us (5%)
  local copies, waits for them, and re-layouts  9.44 us (4%)
  other arithmetic  8.68 us (3%)
    reduce_scatter x1, waiting for transfers between devices, per_device(): lax.psum_scatter(block_sums, 'dp', scatter_dimension=0, tiled=True)  110 us
    all_gather x1, waiting for transfers between devices, per_device(): lax.all_gather(centroids, 'dp', axis=1, tiled=True)[0]  39 us
    all_to_all x1, waiting for transfers between devices, per_device(): lax.all_to_all(outgoing, 'cent', split_axis=0, concat_axis=0, tiled=True)  22.4 us
    all_to_all x1, starting transfers between devices, per_device(): lax.all_to_all(outgoing, 'cent', split_axis=0, concat_axis=0, tiled=True)  9.52 us
    dot_general x1, matrix products, per_device(): lax.dot_general(shares, widened, (((0,), (0,)), ((), ())), preferred_elem...  7.39 us
    all_to_all x1, starting transfers between devices, per_device(): lax.all_to_all(stats, 'cent', split_axis=0, concat_axis=0, tiled=True)  7.25 us
    dot_general x1, matrix products, per_device(): lax.dot_general(incoming, lax.all_gather(centroids, 'dp', axis=1, tiled=T...  5.98 us
    all_to_all x1, starting transfers between devices, per_device(): lax.all_to_all(slot_norms.reshape(owners, slot_rows), 'cent', split_axis=...  5.6 us
  transfers between devices with their start and end apart: 5, of which 5 were waited for; matrix products, arithmetic and copies ran while one was open for 3% of the time, Pallas kernels for 0%

commit v1 on v0

--- a/solution.py
+++ b/solution.py
@@ -1,12 +1,27 @@
+import functools
 import math
 import jax
 import jax.numpy as jnp
 from jax import lax
 from jax.sharding import PartitionSpec as P
+from jax.lax import all_to_all, axis_size
 
 score_scale = 2.0
 prior_weight = 1.0
 empty_norm = 1e30
+
+
+def define_the_area(load, which_dim):
+    block_now = jnp.concatenate(
+        all_to_all(
+            jnp.stack([load] * axis_size("dp")), axis_name="dp", split_axis=0, concat_axis=0
+        ),
+        axis=which_dim,
+    )
+    return block_now
+
+
+view_ratios_up = functools.partial(define_the_area, which_dim=1)
 
 
 def combine_norms(peaks, totals, usable):
@@ -49,7 +64,7 @@
     logits = (
         lax.dot_general(
             incoming,
-            lax.all_gather(centroids, "dp", axis=1, tiled=True)[0],
+            view_ratios_up(centroids)[0],
             (((1,), (1,)), ((), ())),
             preferred_element_type=jnp.float32,
         )

time: 251 us -> 323 us (1.29)
  the two profiles are of different devices: /device:TPU:4 before, /device:TPU:2 now
where the time goes in v1:
time: 323 us; the launch traced here: 322 us
  waiting for transfers between devices  215 us (67%)
  blocking collectives  34.7 us (11%)
  starting transfers between devices  25 us (8%)
  matrix products  14.2 us (4%)
  between operations  13.6 us (4%)
  local copies, waits for them, and re-layouts  11 us (3%)
  other arithmetic  8.68 us (3%)
    reduce_scatter x1, waiting for transfers between devices, per_device(): lax.psum_scatter(block_sums, 'dp', scatter_dimension=0, tiled=True)  105 us
    all_to_all x1, waiting for transfers between devices, define_the_area(): all_to_all(jnp.stack([load] * axis_size('dp')), axis_name='dp', split_axi...  97.7 us
    all_to_all x1, blocking collectives, per_device(): lax.all_to_all(outgoing, 'cent', split_axis=0, concat_axis=0, tiled=True)  34.7 us
    all_to_all x1, starting transfers between devices, define_the_area(): all_to_all(jnp.stack([load] * axis_size('dp')), axis_name='dp', split_axi...  15.6 us
    dot_general x1, matrix products, per_device(): lax.dot_general(shares, widened, (((0,), (0,)), ((), ())), preferred_elem...  7.39 us
  transfers between devices with their start and end apart: 4, of which 4 were waited for; matrix products, arithmetic and copies ran while one was open for 1% of the time, Pallas kernels for 0%

profile of v1, /device:TPU:2, one launch (start us, length us, event | category | flops | bytes accessed | tf_op | source)
XLA Modules:
  0.0 322.3 jit_solution(8725182225531531367)
XLA Ops:
  6.5 0.7 iota_compare_fusion.1
  7.4 0.8 fusion.14
  8.3 1.3 reshape.117
  9.6 0.7 convolution_convert_fusion
  10.3 2.4 reshape.118
  12.7 34.7 %all_to_all.24 = bf16[16,64,1024]{2,1,0:T(8,128)(2,1)S(1)} all-to-all(bf16[16,64,1024]{2,1,0:T(8,128)(2,1)} %reshape.118), channel_id=1, replica_groups=mesh['dp'=32,'cent'=16] {'cent'}, dimensions={0} | all-to-all | bytes 4194304 | tf_op jit(solution)/shard_map/all_to_all | solution.py:62
  47.4 1.6 stack.4
  48.9 15.6 %all-to-all-start.1 = ((bf16[32,1,32,1024]{3,2,1,0:T(8,128)(2,1)}), bf16[32,1,32,1024]{3,2,1,0:T(8,128)(2,1)}, u32[]{:S(2)}, u32[]{:S(2)}) async-start(bf16[32,1,32,1024]{3,2,1,0:T(8,128)(2,1)} %stack.4), calls=%async_computation.1 | async-start | bytes 4194304 | tf_op jit(solution)/shard_map/all_to_all | solution.py:16
  64.9 0.7 gather_fusion.2
  66.0 97.7 %all-to-all-done.1 = bf16[32,1,32,1024]{3,2,1,0:T(8,128)(2,1)} async-done(((bf16[32,1,32,1024]{3,2,1,0:T(8,128)(2,1)}), bf16[32,1,32,1024]{3,2,1,0:T(8,128)(2,1)}, u32[]{:S(2)}, u32[]{:S(2)}) %all-to-all-start.1) | async-done | bytes 2097184 | tf_op jit(solution)/shard_map/all_to_all | solution.py:16
  163.7 6.0 %multiply_reduce_fusion = (f32[1024]{0:T(1024)S(1)}, f32[1024,1024]{0,1:T(8,128)}) fusion(bf16[1024,1024]{1,0:T(8,128)(2,1)S(1)} %bitcast.21, bf16[1024,1024]{1,0:T(8,128)(2,1)} %bitcast.5), kind=kOutput, calls=%fused_computation.6 | convolution fusion | flops 2149579776 | bytes 8392704 | tf_op jit(solution)/shard_map/dot_general | solution.py:65
  169.8 2.9 exponential_reduce_fusion
  172.8 0.7 reshape.173
  173.5 4.7 %all-to-all-start.2 = ((f32[16,1,128]{2,1,0:T(1,128)}), f32[16,1,128]{2,1,0:T(1,128)S(1)}, u32[]{:S(2)}, u32[]{:S(2)}) async-start(f32[16,1,128]{2,1,0:T(1,128)} %reshape.173), calls=%async_computation.2 | async-start | bytes 16384 | tf_op jit(solution)/shard_map/all_to_all | solution.py:76
  178.5 5.9 %all-to-all-done.2 = f32[16,1,128]{2,1,0:T(1,128)S(1)} async-done(((f32[16,1,128]{2,1,0:T(1,128)}), f32[16,1,128]{2,1,0:T(1,128)S(1)}, u32[]{:S(2)}, u32[]{:S(2)}) %all-to-all-start.2) | async-done | bytes 8224 | tf_op jit(solution)/shard_map/all_to_all | solution.py:76
  184.9 0.7 reduce.15
  187.4 0.7 all_to_all.18
  188.1 4.7 %all-to-all-start.3 = ((f32[16,1,64]{2,1,0:T(1,128)}), f32[16,1,64]{2,1,0:T(1,128)S(1)}, u32[]{:S(2)}, u32[]{:S(2)}) async-start(f32[16,1,64]{2,1,0:T(1,128)} %bitcast.8), calls=%async_computation.3 | async-start | bytes 16384 | tf_op jit(solution)/shard_map/all_to_all | solution.py:85
  192.9 6.1 %all-to-all-done.3 = f32[16,1,64]{2,1,0:T(1,128)S(1)} async-done(((f32[16,1,64]{2,1,0:T(1,128)}), f32[16,1,64]{2,1,0:T(1,128)S(1)}, u32[]{:S(2)}, u32[]{:S(2)}) %all-to-all-start.3) | async-done | bytes 4128 | tf_op jit(solution)/shard_map/all_to_all | solution.py:85
  199.5 0.7 reduce.14
  200.3 7.4 %fusion = f32[1024,1152]{1,0:T(8,128)} fusion(bf16[1024,1024]{1,0:T(8,128)(2,1)S(1)} %bitcast.22, f32[1024,1024]{0,1:T(8,128)} %get-tuple-element.10, f32[1024]{0:T(1024)S(1)} %sub.54, bf16[1152]{0:T(1024)(128)(2,1)S(1)} %pad.1.clone), kind=kOutput, calls=%fused_computation.7 | convolution fusion | flops 2423783424 | bytes 11016448 | tf_op jit(solution)/shard_map/dot_general | solution.py:94
  207.7 105.4 %reduce-scatter.2.cloned.1.call-done = f32[32,1152]{1,0:T(8,128)} async-done(((f32[1024,1152]{1,0:T(8,128)}), f32[32,1152]{1,0:T(8,128)}) %reduce-scatter.2.cloned.1.call-update) | async-done | bytes 147472 | tf_op jit(solution)/shard_map/reduce_scatter | solution.py:97
  313.0 0.8 fusion.8
  313.9 1.6 fusion.7
  (52 shorter events, 4.4 us)
Async XLA Ops:
  10.3 37.1 %copy-start = (bf16[1,32,1024]{2,1,0:T(8,128)(2,1)S(1)}, bf16[1,32,1024]{2,1,0:T(8,128)(2,1)}, u32[]{:S(2)}) copy-start(bf16[1,32,1024]{2,1,0:T(8,128)(2,1)} %param.7) | copy-start | bytes 196612
  47.4 17.1 %copy-start.1 = (s32[8,3]{0,1:T(4,128)S(1)}, s32[8,3]{0,1:T(4,128)}, u32[]{:S(2)}) copy-start(s32[8,3]{0,1:T(4,128)} %param.5) | copy-start | bytes 292
  48.9 16.8 %copy-start.2 = (s32[8]{0:T(128)S(1)}, s32[8]{0:T(128)}, u32[]{:S(2)}) copy-start(s32[8]{0:T(128)} %param.6) | copy-start | bytes 100
  48.9 114.8 %all-to-all-start.1 = ((bf16[32,1,32,1024]{3,2,1,0:T(8,128)(2,1)}), bf16[32,1,32,1024]{3,2,1,0:T(8,128)(2,1)}, u32[]{:S(2)}, u32[]{:S(2)}) async-start(bf16[32,1,32,1024]{3,2,1,0:T(8,128)(2,1)} %stack.4), calls=%async_computation.1 | async-start | bytes 4194304 | tf_op jit(solution)/shard_map/all_to_all | solution.py:16
  173.5 10.9 %all-to-all-start.2 = ((f32[16,1,128]{2,1,0:T(1,128)}), f32[16,1,128]{2,1,0:T(1,128)S(1)}, u32[]{:S(2)}, u32[]{:S(2)}) async-start(f32[16,1,128]{2,1,0:T(1,128)} %reshape.173), calls=%async_computation.2 | async-start | bytes 16384 | tf_op jit(solution)/shard_map/all_to_all | solution.py:76
  188.1 10.9 %all-to-all-start.3 = ((f32[16,1,64]{2,1,0:T(1,128)}), f32[16,1,64]{2,1,0:T(1,128)S(1)}, u32[]{:S(2)}, u32[]{:S(2)}) async-start(f32[16,1,64]{2,1,0:T(1,128)} %bitcast.8), calls=%async_computation.3 | async-start | bytes 16384 | tf_op jit(solution)/shard_map/all_to_all | solution.py:85
  192.8 120.2 %reduce-scatter.2.cloned.1.call-start = ((), (), s32[]{:S(2)}) async-start(), calls=%async_computation.5 | async-start | bytes 4866048 | tf_op jit(solution)/shard_map/reduce_scatter | solution.py:97
Sparse Core Ops, SparseCore 0:
  207.8 105.1 reduce-scatter.1
